TPU v7x, 256 devices: a whole 4x4x8 slice. The times are simulated.
256 devices in a mesh: seq: 64 (over y, z, core), tr: 2 (over x_lo), tc: 2 (over x_hi).
Axes of the slice: x: 4 (x_hi: 2, x_lo: 2; x = x_hi * 2 + x_lo), y: 4, z: 8, core: 2. Of those that a mesh axis runs over, the one named last changes fastest.
Arguments:
- activations: bfloat16 [65536, 1024], P('seq', ('tr', 'tc')), may hold values from -6 to 6
- seg_len: int32 [64], P('seq'), may hold values from 1 to 1024, as said below
- seg_start: int32 [64], P('seq'), may hold values from 0 to 1, as said below
- memory_rates: float32 [3, 64, 8], P(None, 'seq'), may hold values from 0 to 1, as said below
- w_qkv: bfloat16 [1024, 3, 1024], P(None, None, ('tr', 'tc')), may hold values from -0.1875 to 0.1875
- conv_w: float32 [4, 3, 1024], P(None, None, ('tr', 'tc')), may hold values from -3 to 3
- persistent: bfloat16 [2, 16, 1024], P(None, None, ('tr', 'tc')), may hold values from -6 to 6
- w_out: bfloat16 [1024, 1024], P(('tr', 'tc')), may hold values from -0.1875 to 0.1875
- w_gate: bfloat16 [1024, 2816], P(None, ('tr', 'tc')), may hold values from -0.1875 to 0.1875
- w_up: bfloat16 [1024, 2816], P(None, ('tr', 'tc')), may hold values from -0.1875 to 0.1875
- w_down: bfloat16 [2816, 1024], P(('tr', 'tc')), may hold values from -0.109375 to 0.109375
Outputs:
- layer_out: bfloat16 [65536, 1024], P('seq', ('tr', 'tc'))
Inputs may be any that keep to these rules, and one draw needn't show every extreme that they name: `seg_start`: 1 where a segment begins a prompt, 0 where it continues the prompt of the segment before; segment 0 begins a prompt; a prompt spans at most 32 segments, and in every draw one prompt spans exactly that many. `seg_len`: live tokens at the head of each segment; every segment of a prompt but its last is full. `memory_rates`: all three tables lie strictly between 0 and 1.
All inputs are finite; a program needn't handle non-finite values.
Results may differ from a plain program's by a relative error of at most 0.015.
Values may be sent and summed in bfloat16 or wider, within the bound.
No kernel may reach another device: no remote copies, remote signals or barrier semaphores. Data moves between devices by JAX's collectives and lax.ppermute only.
A program may use at most 192 MiB of HBM per device.

v0:
```python
import jax
import jax.numpy as jnp
from jax import lax
from jax.sharding import PartitionSpec as P

HD = 128
SEG = 1024
CONV = 4
PROMPT_SPAN = 32
epsilon = 1e-06
score_scale = 8.0


def passed_along(block, axis, distance):
    devices = range(lax.axis_size(axis))
    route = [(i - distance, i) for i in devices if i - distance in devices]
    return lax.ppermute(block, axis, route)


def passed_exact(block, axis, distance):
    high = block.astype(jnp.bfloat16)
    low = (block - high.astype(jnp.float32)).astype(jnp.bfloat16)
    high, low = passed_along((high, low), axis, distance)
    return high.astype(jnp.float32) + low.astype(jnp.float32)


def window_scan(seg_map, seg_shift, axis, reach):
    distance = 1
    while distance < reach:
        if 2 * distance >= reach:
            shift_before = passed_exact(seg_shift, axis, distance)
            seg_shift = exact_product(seg_map, shift_before) + seg_shift
        else:
            high = seg_shift.astype(jnp.bfloat16)
            low = (seg_shift - high.astype(jnp.float32)).astype(jnp.bfloat16)
            map_before, high, low = passed_along(
                (seg_map.astype(jnp.bfloat16), high, low), axis, distance
            )
            shift_before = high.astype(jnp.float32) + low.astype(jnp.float32)
            seg_shift = exact_product(seg_map, shift_before) + seg_shift
            seg_map = exact_product(seg_map, map_before.astype(jnp.float32))
        distance *= 2
    return seg_shift


def unit_rows(values_in):
    return values_in * lax.rsqrt(jnp.sum(values_in * values_in, -1, keepdims=True) + epsilon)


def exact_product(left, right):
    return jnp.matmul(left, right, precision=lax.Precision.HIGHEST)


def body(
    activations,
    seg_len,
    seg_start,
    memory_rates,
    w_qkv,
    conv_w,
    persistent,
    w_out,
    w_gate,
    w_up,
    w_down,
):
    token_rows, local_feat = activations.shape
    seg_count = seg_len.shape[0]
    full_width = w_qkv.shape[0]
    head_width = w_qkv.shape[2]
    local_heads = head_width // HD
    group_index = lax.axis_index(("tr", "tc"))
    wide = w_qkv.reshape(full_width, 3 * head_width)
    row_ids = jnp.arange(token_rows, dtype=jnp.int32)
    position = row_ids % SEG
    segment_of = row_ids // SEG
    continuing = seg_start[segment_of] == 0
    piece = lax.all_gather(activations, ("tr", "tc"), axis=1, tiled=True)
    piece_f = piece.astype(jnp.float32)
    projected = jnp.dot(piece, wide, preferred_element_type=jnp.float32)
    squares = jnp.sum(piece_f * piece_f, -1)
    qkv = (projected * lax.rsqrt(squares / full_width + epsilon)[:, None]).astype(jnp.bfloat16)
    edge_rows = passed_along(qkv[token_rows - (CONV - 1) :], "seq", 1)
    extended = jnp.concatenate([edge_rows, qkv], 0)
    taps = conv_w.reshape(CONV, 3 * head_width)
    convolved = jnp.zeros((token_rows, 3 * head_width), jnp.float32)
    for offset in range(CONV):
        shifted = extended[CONV - 1 - offset : CONV - 1 - offset + token_rows].astype(jnp.float32)
        valid = (position >= offset) | continuing
        convolved = convolved + jnp.where(valid[:, None], taps[offset] * shifted, 0.0)
    parts = convolved.reshape(token_rows, 3, local_heads, HD)
    query_n = unit_rows(parts[:, 0]).astype(jnp.bfloat16)
    key_n = unit_rows(parts[:, 1]).astype(jnp.bfloat16)
    value_n = parts[:, 2].astype(jnp.bfloat16)
    pkeys = unit_rows(persistent[0].astype(jnp.float32).reshape(-1, local_heads, HD)).astype(
        jnp.bfloat16
    )
    pvalues = persistent[1].reshape(-1, local_heads, HD)
    persist_rows = pkeys.shape[0]
    live = position < seg_len[segment_of]
    keys_live = jnp.where(live[:, None, None], key_n, jnp.zeros((), jnp.bfloat16)).reshape(
        seg_count, SEG, local_heads, HD
    )
    value_segs = value_n.reshape(seg_count, SEG, local_heads, HD)
    a_mats = jnp.einsum("cthi,cthj->chij", keys_live, keys_live, preferred_element_type=jnp.float32)
    b_mats = jnp.einsum(
        "cthi,cthj->chij", keys_live, value_segs, preferred_element_type=jnp.float32
    )
    my_rates = lax.dynamic_slice_in_dim(memory_rates, group_index * local_heads, local_heads, 2)
    decay_factor = my_rates[0][:, :, None, None]
    eta = my_rates[1][:, :, None, None]
    theta = my_rates[2][:, :, None, None]
    keep = (1 - seg_start).astype(jnp.float32)[:, None, None, None]
    identity = jnp.eye(HD, dtype=jnp.float32)
    upper = jnp.concatenate([(1.0 - decay_factor) * identity - theta * a_mats, eta * identity], -1)
    lower = jnp.concatenate([-theta * a_mats, eta * identity], -1)
    seg_maps = jnp.concatenate([upper, lower], -2) * keep
    seg_shifts = jnp.concatenate([theta * b_mats, theta * b_mats], -2)
    reach = min(PROMPT_SPAN, lax.axis_size("seq"))
    state_out = window_scan(seg_maps[0], seg_shifts[0], "seq", reach)
    memory_in = passed_exact(state_out[:, :HD], "seq", 1) * keep[0]
    query_seg = query_n.astype(jnp.float32)
    retr_parts = jnp.einsum("thi,hij->thj", query_seg, memory_in, precision=lax.Precision.HIGHEST)
    mem = retr_parts * lax.rsqrt(jnp.mean(retr_parts * retr_parts, -1, keepdims=True) + epsilon)
    block_rows = min(512, SEG)
    attn_parts = []
    seg_index = 0
    first = seg_index * SEG
    keys_all = jnp.concatenate([pkeys, key_n], 0)
    values_all = jnp.concatenate([pvalues, value_n], 0)
    cols_k = jnp.arange(persist_rows + SEG, dtype=jnp.int32)[None, :] - persist_rows
    for block_start in range(0, SEG, block_rows):
        query_blk = query_n[first + block_start : first + block_start + block_rows]
        scores = score_scale * jnp.einsum(
            "qhd,khd->hqk", query_blk, keys_all, preferred_element_type=jnp.float32
        )
        rows_q = block_start + jnp.arange(block_rows, dtype=jnp.int32)[:, None]
        allow = (cols_k < 0) | (cols_k <= rows_q) & (cols_k < seg_len[seg_index])
        weights = jnp.where(allow[None], jnp.exp(scores), 0.0)
        probs = (weights / jnp.sum(weights, -1, keepdims=True)).astype(jnp.bfloat16)
        attn_parts.append(
            jnp.einsum("hqk,khd->qhd", probs, values_all, preferred_element_type=jnp.float32)
        )
    attn = jnp.concatenate(attn_parts, 0)
    heads_out = (attn + mem).astype(jnp.bfloat16).reshape(token_rows, head_width)
    partial_value = jnp.dot(heads_out, w_out, preferred_element_type=jnp.float32)
    share = lax.psum_scatter(
        partial_value.astype(jnp.bfloat16), ("tr", "tc"), scatter_dimension=1, tiled=True
    ).astype(jnp.float32)
    resid = (activations.astype(jnp.float32) + share).astype(jnp.bfloat16)
    piece = lax.all_gather(resid, ("tr", "tc"), axis=1, tiled=True)
    piece_f = piece.astype(jnp.float32)
    gate = jnp.dot(piece, w_gate, preferred_element_type=jnp.float32)
    up_proj = jnp.dot(piece, w_up, preferred_element_type=jnp.float32)
    squares2 = jnp.sum(piece_f * piece_f, -1)
    inv_rms2 = lax.rsqrt(squares2 / full_width + epsilon)[:, None]
    hidden = (jax.nn.silu(gate * inv_rms2) * (up_proj * inv_rms2)).astype(jnp.bfloat16)
    down = jnp.dot(hidden, w_down, preferred_element_type=jnp.float32)
    ffn_share = lax.psum_scatter(
        down.astype(jnp.bfloat16), ("tr", "tc"), scatter_dimension=1, tiled=True
    ).astype(jnp.float32)
    return (resid.astype(jnp.float32) + ffn_share).astype(jnp.bfloat16)


def solution(mesh):
    return jax.shard_map(
        body,
        mesh=mesh,
        in_specs=(
            P("seq", ("tr", "tc")),
            P("seq"),
            P("seq"),
            P(None, "seq", None),
            P(None, None, ("tr", "tc")),
            P(None, None, ("tr", "tc")),
            P(None, None, ("tr", "tc")),
            P(("tr", "tc"), None),
            P(None, ("tr", "tc")),
            P(None, ("tr", "tc")),
            P(("tr", "tc"), None),
        ),
        out_specs=P("seq", ("tr", "tc")),
        check_vma=False,
    )
```

profile of v0, /device:TPU:1, one launch (start us, length us, event | category | flops | bytes accessed | tf_op | source)
XLA Modules:
  0.0 371.0 jit_solution(2655117677076065765)
XLA Ops:
  9.5 2.6 copy.76
  16.3 46.8 %all-gather.3.cloned.1.call-done = bf16[1024,1024]{1,0:T(8,128)(2,1)} async-done(((bf16[1024,256]{1,0:T(8,128)(2,1)}), bf16[1024,1024]{1,0:T(8,128)(2,1)}) %all-gather.3.cloned.1.call-update) | async-done | bytes 2097168 | tf_op jit(solution)/shard_map/all_gather | solution.py:78
  63.1 2.1 multiply_reduce_fusion.1
  65.2 3.9 %multiply_convert_fusion = bf16[1024,768]{1,0:T(8,128)(2,1)S(1)} fusion(bf16[1024,1024]{1,0:T(8,128)(2,1)} %all-gather.3.cloned.1.call-done, bf16[1024,768]{0,1:T(8,128)(2,1)} %bitcast.82, f32[1024]{0:T(1024)S(1)} %add_rsqrt_fusion.4), kind=kOutput, calls=%fused_computation.11 | convolution fusion | flops 1612185600 | bytes 5246976 | tf_op jit(solution)/shard_map/dot_general | solution.py:80
  69.1 3.6 collective-permute-start
  73.5 3.8 %select_add_fusion = f32[1024,768]{1,0:T(8,128)} fusion(bf16[1024,768]{1,0:T(8,128)(2,1)S(1)} %multiply_convert_fusion, bf16[3,768]{1,0:T(4,128)(2,1)S(1)} %collective-permute-done, f32[768]{0:T(1024)S(1)} %mul.251, f32[768]{0:T(1024)S(1)} %mul.248, f32[768]{0:T(1024)S(1)} %mul.245, f32[768]{0:T(1024)S(1)} %mul.239, ...), kind=kLoop, calls=%fused_computation.10 | loop fusion | flops 18874368 | bytes 4739584 | tf_op jit(solution)/shard_map/add | solution.py:90
  77.3 5.2 %reshape.298 = f32[1024,3,2,128]{3,2,1,0:T(2,128)} reshape(f32[1024,768]{1,0:T(8,128)} %select_add_fusion) | data formatting | bytes 6291456 | tf_op jit(solution)/shard_map/reshape | solution.py:91
  88.6 4.2 %collective-permute-start.5 = (bf16[2,256,128]{1,2,0:T(8,128)(2,1)}, bf16[2,256,128]{1,2,0:T(8,128)(2,1)}, u32[]{:S(2)}, u32[]{:S(2)}) collective-permute-start(bf16[2,256,128]{1,2,0:T(8,128)(2,1)} %fusion.24), channel_id=1, source_target_pairs={{0,4},{4,8},{8,12},{12,16},{16,20},{20,24},{24,28},{28,32},{32,36}... | collective-permute-start | bytes 393224 | tf_op jit(solution)/shard_map/ppermute | solution.py:17
  96.2 3.5 collective-permute-start.1
  99.8 3.0 fusion.3
  102.8 2.9 fusion.1
  105.7 4.5 %fusion.12 = f32[512,2,128]{0,2,1:T(8,128)S(1)} fusion(f32[2,512,1040]{1,2,0:T(8,128)} %fusion.3, bf16[1024,2,128]{2,0,1:T(8,128)(2,1)} %bitcast.84, bf16[16,2,128]{2,0,1:T(8,128)(2,1)S(1)} %copy.78), kind=kOutput, calls=%fused_computation.29 | convolution fusion | flops 275826688 | bytes 5316608 | tf_op jit(solution)/shard_map/hqk,khd->qhd/dot_general | solution.py:142
  111.8 3.2 collective-permute-start.8
  115.0 5.8 %collective-permute-start.7 = (bf16[2,256,128]{1,2,0:T(8,128)(2,1)S(1)}, bf16[2,256,128]{1,2,0:T(8,128)(2,1)S(1)}, u32[]{:S(2)}, u32[]{:S(2)}) collective-permute-start(bf16[2,256,128]{1,2,0:T(8,128)(2,1)S(1)} %get-tuple-element.18), channel_id=1, source_target_pairs={{0,8},{4,12},{8,16},{12,20},{16,24},{20,28},{24,32},{28,36},{32,40... | collective-permute-start | bytes 393224 | tf_op jit(solution)/shard_map/ppermute | solution.py:17
  124.1 3.5 collective-permute-start.10
  127.6 3.6 collective-permute-start.9
  131.6 2.3 collective-permute-start.3
  133.8 5.3 %collective-permute-done.9 = bf16[2,256,128]{1,2,0:T(8,128)(2,1)S(1)} collective-permute-done((bf16[2,256,128]{1,2,0:T(8,128)(2,1)S(1)}, bf16[2,256,128]{1,2,0:T(8,128)(2,1)S(1)}, u32[]{:S(2)}, u32[]{:S(2)}) %collective-permute-start.9) | collective-permute-done | bytes 131104 | tf_op jit(solution)/shard_map/ppermute | solution.py:17
  139.8 8.8 %collective-permute-start.12 = (bf16[2,256,128]{1,2,0:T(8,128)(2,1)S(1)}, bf16[2,256,128]{1,2,0:T(8,128)(2,1)S(1)}, u32[]{:S(2)}, u32[]{:S(2)}) collective-permute-start(bf16[2,256,128]{1,2,0:T(8,128)(2,1)S(1)} %get-tuple-element.13), channel_id=1, source_target_pairs={{0,32},{4,36},{8,40},{12,44},{16,48},{20,52},{24,56},{28,60},{32,6... | collective-permute-start | bytes 393224 | tf_op jit(solution)/shard_map/ppermute | solution.py:17
  148.7 8.0 %collective-permute-start.11 = (bf16[2,256,128]{1,2,0:T(8,128)(2,1)S(1)}, bf16[2,256,128]{1,2,0:T(8,128)(2,1)S(1)}, u32[]{:S(2)}, u32[]{:S(2)}) collective-permute-start(bf16[2,256,128]{1,2,0:T(8,128)(2,1)S(1)} %get-tuple-element.14), channel_id=1, source_target_pairs={{0,32},{4,36},{8,40},{12,44},{16,48},{20,52},{24,56},{28,60},{32,6... | collective-permute-start | bytes 393224 | tf_op jit(solution)/shard_map/ppermute | solution.py:17
  157.1 2.1 collective-permute-start.4
  161.3 6.2 %collective-permute-start.14 = (bf16[2,256,128]{1,2,0:T(8,128)(2,1)S(1)}, bf16[2,256,128]{1,2,0:T(8,128)(2,1)S(1)}, u32[]{:S(2)}, u32[]{:S(2)}) collective-permute-start(bf16[2,256,128]{1,2,0:T(8,128)(2,1)S(1)} %get-tuple-element.11), channel_id=1, source_target_pairs={{0,64},{4,68},{8,72},{12,76},{16,80},{20,84},{24,88},{28,92},{32,9... | collective-permute-start | bytes 393224 | tf_op jit(solution)/shard_map/ppermute | solution.py:17
  167.5 3.4 collective-permute-start.13
  171.3 2.4 collective-permute-done.13
  174.4 4.2 %collective-permute-start.16 = (bf16[2,128,128]{1,2,0:T(8,128)(2,1)S(1)}, bf16[2,128,128]{1,2,0:T(8,128)(2,1)S(1)}, u32[]{:S(2)}, u32[]{:S(2)}) collective-permute-start(bf16[2,128,128]{1,2,0:T(8,128)(2,1)S(1)} %get-tuple-element.9), channel_id=1, source_target_pairs={{0,4},{4,8},{8,12},{12,16},{16,20},{20,24},{24,28},{28,32},{32,36}... | collective-permute-start | bytes 196616 | tf_op jit(solution)/shard_map/ppermute | solution.py:17
  180.6 4.5 %fusion.13 = f32[512,2,128]{0,2,1:T(8,128)S(1)} fusion(f32[2,512,1040]{1,2,0:T(8,128)} %fusion.1, bf16[1024,2,128]{2,0,1:T(8,128)(2,1)} %bitcast.85, bf16[16,2,128]{2,0,1:T(8,128)(2,1)S(1)} %copy.78), kind=kOutput, calls=%fused_computation.30 | convolution fusion | flops 275826688 | bytes 5316608 | tf_op jit(solution)/shard_map/hqk,khd->qhd/dot_general | solution.py:142
  187.7 2.1 convolution_convert_fusion
  189.8 54.3 %reduce-scatter.3.cloned.1.call-done = bf16[1024,256]{1,0:T(8,128)(2,1)} async-done(((bf16[1024,1024]{1,0:T(8,128)(2,1)}), bf16[1024,256]{1,0:T(8,128)(2,1)}) %reduce-scatter.3.cloned.1.call-update) | async-done | bytes 524304 | tf_op jit(solution)/shard_map/reduce_scatter | solution.py:147
  246.4 50.0 %all-gather.5.cloned.1.call-done = bf16[1024,1024]{1,0:T(8,128)(2,1)} async-done(((bf16[1024,256]{1,0:T(8,128)(2,1)}), bf16[1024,1024]{1,0:T(8,128)(2,1)}) %all-gather.5.cloned.1.call-update) | async-done | bytes 2097168 | tf_op jit(solution)/shard_map/all_gather | solution.py:151
  298.5 4.9 %fusion.91 = f32[1024,704]{0,1:T(8,128)} fusion(bf16[1024,1024]{1,0:T(8,128)(2,1)} %all-gather.5.cloned.1.call-done, bf16[1024,704]{0,1:T(8,128)(2,1)S(1)} %copy-done.15), kind=kOutput, calls=%fused_computation.159 | convolution fusion | flops 1476395008 | bytes 6422528 | tf_op jit(solution)/shard_map/dot_general | solution.py:153
  303.4 7.8 %convolution_convert_fusion.1 = bf16[1024,1024]{1,0:T(8,128)(2,1)} fusion(bf16[704,1024]{1,0:T(8,128)(2,1)S(1)} %copy-done, f32[1024,704]{0,1:T(8,128)} %fusion.91, bf16[1024,1024]{1,0:T(8,128)(2,1)} %all-gather.5.cloned.1.call-done, bf16[1024,704]{0,1:T(8,128)(2,1)} %param.20, f32[1024]{0:T(1024)S(1)} %add_rsqrt_fusion.3), kind=kOutput, calls=%fused_computation.22 | convolution fusion | flops 2959605760 | bytes 9965568 | tf_op jit(solution)/shard_map/dot_general | solution.py:158
  311.3 51.2 %reduce-scatter.5.cloned.1.call-done = bf16[1024,256]{1,0:T(8,128)(2,1)} async-done(((bf16[1024,1024]{1,0:T(8,128)(2,1)}), bf16[1024,256]{1,0:T(8,128)(2,1)}) %reduce-scatter.5.cloned.1.call-update) | async-done | bytes 524304 | tf_op jit(solution)/shard_map/reduce_scatter | solution.py:159
  (118 shorter events, 36.0 us)
Async XLA Ops:
  6.5 296.9 %copy-start = (bf16[704,1024]{1,0:T(8,128)(2,1)S(1)}, bf16[704,1024]{1,0:T(8,128)(2,1)}, u32[]{:S(2)}) copy-start(bf16[704,1024]{1,0:T(8,128)(2,1)} %param.21) | copy-start | bytes 4325380
  6.5 6.9 %copy-start.10 = (f32[4,3,256]{2,0,1:T(4,128)S(1)}, f32[4,3,256]{2,0,1:T(4,128)}, u32[]{:S(2)}) copy-start(f32[4,3,256]{2,0,1:T(4,128)} %param.16) | copy-start | bytes 36868
  6.5 56.6 %all-gather.3.cloned.1.call-start = ((), (), s32[]{:S(2)}) async-start(), calls=%async_computation.2 | async-start | bytes 2621440 | tf_op jit(solution)/shard_map/all_gather | solution.py:78
  7.3 236.9 %reduce-scatter.3.cloned.1.call-start = ((), (), s32[]{:S(2)}) async-start(), calls=%async_computation.3 | async-start | bytes 2621440 | tf_op jit(solution)/shard_map/reduce_scatter | solution.py:147
  13.5 55.6 %copy-start.8 = (f32[128,128]{0,1:T(8,128)}, f32[128,128]{0,1:T(8,128)S(1)}, u32[]{:S(2)}) copy-start(f32[128,128]{0,1:T(8,128)S(1)} %fusion.50) | copy-start | bytes 196612
  69.1 4.4 %collective-permute-start = (bf16[3,768]{1,0:T(4,128)(2,1)S(1)}, bf16[3,768]{1,0:T(4,128)(2,1)S(1)}, u32[]{:S(2)}, u32[]{:S(2)}) collective-permute-start(bf16[3,768]{1,0:T(4,128)(2,1)S(1)} %slice.81), channel_id=1, source_target_pairs={{0,4},{4,8},{8,12},{12,16},{16,20},{20,24},{24,28},{28,32},{32,36}... | collective-permute-start | bytes 13832 | tf_op jit(solution)/shard_map/ppermute | solution.py:17
  86.3 8.5 %copy-start.9 = (f32[128,128]{0,1:T(8,128)S(1)}, f32[128,128]{0,1:T(8,128)}, u32[]{:S(2)}) copy-start(f32[128,128]{0,1:T(8,128)} %copy-done.8) | copy-start | bytes 196612
  86.3 8.5 %copy-start.12 = (f32[2]{0:T(128)S(1)}, f32[2]{0:T(128)}, u32[]{:S(2)}) copy-start(f32[2]{0:T(128)} %get-tuple-element.19) | copy-start | bytes 28
  86.3 8.5 %copy-start.14 = (f32[2]{0:T(128)S(1)}, f32[2]{0:T(128)}, u32[]{:S(2)}) copy-start(f32[2]{0:T(128)} %get-tuple-element.31) | copy-start | bytes 28
  86.7 8.7 %copy-start.5 = (f32[1,2,128,128]{2,3,1,0:T(8,128)S(1)}, f32[1,2,128,128]{2,3,1,0:T(8,128)}, u32[]{:S(2)}) copy-start(f32[1,2,128,128]{2,3,1,0:T(8,128)} %broadcast_multiply_fusion) | copy-start | bytes 393220
  87.9 11.9 %copy-start.4 = (pred[512,1040]{0,1:T(8,128)(4,1)S(1)}, pred[512,1040]{0,1:T(8,128)(4,1)}, u32[]{:S(2)}) copy-start(pred[512,1040]{0,1:T(8,128)(4,1)} %get-tuple-element.30) | copy-start | bytes 1597444
  88.6 21.7 %collective-permute-start.5 = (bf16[2,256,128]{1,2,0:T(8,128)(2,1)}, bf16[2,256,128]{1,2,0:T(8,128)(2,1)}, u32[]{:S(2)}, u32[]{:S(2)}) collective-permute-start(bf16[2,256,128]{1,2,0:T(8,128)(2,1)} %fusion.24), channel_id=1, source_target_pairs={{0,4},{4,8},{8,12},{12,16},{16,20},{20,24},{24,28},{28,32},{32,36}... | collective-permute-start | bytes 393224 | tf_op jit(solution)/shard_map/ppermute | solution.py:17
  92.8 17.5 %collective-permute-start.6 = (bf16[2,256,128]{1,2,0:T(8,128)(2,1)S(1)}, bf16[2,256,128]{1,2,0:T(8,128)(2,1)}, u32[]{:S(2)}, u32[]{:S(2)}) collective-permute-start(bf16[2,256,128]{1,2,0:T(8,128)(2,1)S(1)} %fusion.25), channel_id=1, source_target_pairs={{0,4},{4,8},{8,12},{12,16},{16,20},{20,24},{24,28},{28,32},{32,36}... | collective-permute-start | bytes 393224 | tf_op jit(solution)/shard_map/ppermute | solution.py:17
  96.2 24.6 %collective-permute-start.1 = (bf16[2,256,256]{1,2,0:T(8,128)(2,1)}, bf16[2,256,256]{1,2,0:T(8,128)(2,1)S(1)}, u32[]{:S(2)}, u32[]{:S(2)}) collective-permute-start(bf16[2,256,256]{1,2,0:T(8,128)(2,1)} %fusion.18), channel_id=1, source_target_pairs={{0,4},{4,8},{8,12},{12,16},{16,20},{20,24},{24,28},{28,32},{32,36}... | collective-permute-start | bytes 786440 | tf_op jit(solution)/shard_map/ppermute | solution.py:17
  111.8 11.6 %collective-permute-start.8 = (bf16[2,256,128]{1,2,0:T(8,128)(2,1)S(1)}, bf16[2,256,128]{1,2,0:T(8,128)(2,1)S(1)}, u32[]{:S(2)}, u32[]{:S(2)}) collective-permute-start(bf16[2,256,128]{1,2,0:T(8,128)(2,1)S(1)} %get-tuple-element.17), channel_id=1, source_target_pairs={{0,8},{4,12},{8,16},{12,20},{16,24},{20,28},{24,32},{28,36},{32,40... | collective-permute-start | bytes 393224 | tf_op jit(solution)/shard_map/ppermute | solution.py:17
  115.0 8.4 %collective-permute-start.7 = (bf16[2,256,128]{1,2,0:T(8,128)(2,1)S(1)}, bf16[2,256,128]{1,2,0:T(8,128)(2,1)S(1)}, u32[]{:S(2)}, u32[]{:S(2)}) collective-permute-start(bf16[2,256,128]{1,2,0:T(8,128)(2,1)S(1)} %get-tuple-element.18), channel_id=1, source_target_pairs={{0,8},{4,12},{8,16},{12,20},{16,24},{20,28},{24,32},{28,36},{32,40... | collective-permute-start | bytes 393224 | tf_op jit(solution)/shard_map/ppermute | solution.py:17
  121.4 9.7 %collective-permute-start.2 = (bf16[2,256,256]{2,1,0:T(8,128)(2,1)S(1)}, bf16[2,256,256]{2,1,0:T(8,128)(2,1)S(1)}, u32[]{:S(2)}, u32[]{:S(2)}) collective-permute-start(bf16[2,256,256]{2,1,0:T(8,128)(2,1)S(1)} %get-tuple-element.34), channel_id=1, source_target_pairs={{0,8},{4,12},{8,16},{12,20},{16,24},{20,28},{24,32},{28,36},{32,40... | collective-permute-start | bytes 786440 | tf_op jit(solution)/shard_map/ppermute | solution.py:17
  124.1 9.8 %collective-permute-start.10 = (bf16[2,256,128]{1,2,0:T(8,128)(2,1)S(1)}, bf16[2,256,128]{1,2,0:T(8,128)(2,1)S(1)}, u32[]{:S(2)}, u32[]{:S(2)}) collective-permute-start(bf16[2,256,128]{1,2,0:T(8,128)(2,1)S(1)} %get-tuple-element.15), channel_id=1, source_target_pairs={{0,16},{4,20},{8,24},{12,28},{16,32},{20,36},{24,40},{28,44},{32,4... | collective-permute-start | bytes 393224 | tf_op jit(solution)/shard_map/ppermute | solution.py:17
  127.6 11.6 %collective-permute-start.9 = (bf16[2,256,128]{1,2,0:T(8,128)(2,1)S(1)}, bf16[2,256,128]{1,2,0:T(8,128)(2,1)S(1)}, u32[]{:S(2)}, u32[]{:S(2)}) collective-permute-start(bf16[2,256,128]{1,2,0:T(8,128)(2,1)S(1)} %get-tuple-element.16), channel_id=1, source_target_pairs={{0,16},{4,20},{8,24},{12,28},{16,32},{20,36},{24,40},{28,44},{32,4... | collective-permute-start | bytes 393224 | tf_op jit(solution)/shard_map/ppermute | solution.py:17
  131.6 25.2 %collective-permute-start.3 = (bf16[2,256,256]{2,1,0:T(8,128)(2,1)S(1)}, bf16[2,256,256]{2,1,0:T(8,128)(2,1)S(1)}, u32[]{:S(2)}, u32[]{:S(2)}) collective-permute-start(bf16[2,256,256]{2,1,0:T(8,128)(2,1)S(1)} %get-tuple-element.37), channel_id=1, source_target_pairs={{0,16},{4,20},{8,24},{12,28},{16,32},{20,36},{24,40},{28,44},{32,4... | collective-permute-start | bytes 786440 | tf_op jit(solution)/shard_map/ppermute | solution.py:17
  139.8 19.4 %collective-permute-start.12 = (bf16[2,256,128]{1,2,0:T(8,128)(2,1)S(1)}, bf16[2,256,128]{1,2,0:T(8,128)(2,1)S(1)}, u32[]{:S(2)}, u32[]{:S(2)}) collective-permute-start(bf16[2,256,128]{1,2,0:T(8,128)(2,1)S(1)} %get-tuple-element.13), channel_id=1, source_target_pairs={{0,32},{4,36},{8,40},{12,44},{16,48},{20,52},{24,56},{28,60},{32,6... | collective-permute-start | bytes 393224 | tf_op jit(solution)/shard_map/ppermute | solution.py:17
  148.7 11.9 %collective-permute-start.11 = (bf16[2,256,128]{1,2,0:T(8,128)(2,1)S(1)}, bf16[2,256,128]{1,2,0:T(8,128)(2,1)S(1)}, u32[]{:S(2)}, u32[]{:S(2)}) collective-permute-start(bf16[2,256,128]{1,2,0:T(8,128)(2,1)S(1)} %get-tuple-element.14), channel_id=1, source_target_pairs={{0,32},{4,36},{8,40},{12,44},{16,48},{20,52},{24,56},{28,60},{32,6... | collective-permute-start | bytes 393224 | tf_op jit(solution)/shard_map/ppermute | solution.py:17
  157.1 13.7 %collective-permute-start.4 = (bf16[2,256,256]{2,1,0:T(8,128)(2,1)S(1)}, bf16[2,256,256]{2,1,0:T(8,128)(2,1)S(1)}, u32[]{:S(2)}, u32[]{:S(2)}) collective-permute-start(bf16[2,256,256]{2,1,0:T(8,128)(2,1)S(1)} %get-tuple-element.40), channel_id=1, source_target_pairs={{0,32},{4,36},{8,40},{12,44},{16,48},{20,52},{24,56},{28,60},{32,6... | collective-permute-start | bytes 786440 | tf_op jit(solution)/shard_map/ppermute | solution.py:17
  161.3 10.0 %collective-permute-start.14 = (bf16[2,256,128]{1,2,0:T(8,128)(2,1)S(1)}, bf16[2,256,128]{1,2,0:T(8,128)(2,1)S(1)}, u32[]{:S(2)}, u32[]{:S(2)}) collective-permute-start(bf16[2,256,128]{1,2,0:T(8,128)(2,1)S(1)} %get-tuple-element.11), channel_id=1, source_target_pairs={{0,64},{4,68},{8,72},{12,76},{16,80},{20,84},{24,88},{28,92},{32,9... | collective-permute-start | bytes 393224 | tf_op jit(solution)/shard_map/ppermute | solution.py:17
  167.5 6.2 %collective-permute-start.13 = (bf16[2,256,128]{1,2,0:T(8,128)(2,1)S(1)}, bf16[2,256,128]{1,2,0:T(8,128)(2,1)S(1)}, u32[]{:S(2)}, u32[]{:S(2)}) collective-permute-start(bf16[2,256,128]{1,2,0:T(8,128)(2,1)S(1)} %get-tuple-element.12), channel_id=1, source_target_pairs={{0,64},{4,68},{8,72},{12,76},{16,80},{20,84},{24,88},{28,92},{32,9... | collective-permute-start | bytes 393224 | tf_op jit(solution)/shard_map/ppermute | solution.py:17
  174.4 11.1 %collective-permute-start.16 = (bf16[2,128,128]{1,2,0:T(8,128)(2,1)S(1)}, bf16[2,128,128]{1,2,0:T(8,128)(2,1)S(1)}, u32[]{:S(2)}, u32[]{:S(2)}) collective-permute-start(bf16[2,128,128]{1,2,0:T(8,128)(2,1)S(1)} %get-tuple-element.9), channel_id=1, source_target_pairs={{0,4},{4,8},{8,12},{12,16},{16,20},{20,24},{24,28},{28,32},{32,36}... | collective-permute-start | bytes 196616 | tf_op jit(solution)/shard_map/ppermute | solution.py:17
  178.7 8.1 %collective-permute-start.15 = (bf16[2,128,128]{1,2,0:T(8,128)(2,1)S(1)}, bf16[2,128,128]{1,2,0:T(8,128)(2,1)S(1)}, u32[]{:S(2)}, u32[]{:S(2)}) collective-permute-start(bf16[2,128,128]{1,2,0:T(8,128)(2,1)S(1)} %get-tuple-element.10), channel_id=1, source_target_pairs={{0,4},{4,8},{8,12},{12,16},{16,20},{20,24},{24,28},{28,32},{32,36}... | collective-permute-start | bytes 196616 | tf_op jit(solution)/shard_map/ppermute | solution.py:17
  187.7 56.5 %copy-start.2 = (bf16[1024,256]{1,0:T(8,128)(2,1)S(1)}, bf16[1024,256]{1,0:T(8,128)(2,1)}, u32[]{:S(2)}) copy-start(bf16[1024,256]{1,0:T(8,128)(2,1)} %param.11) | copy-start | bytes 1572868
  189.8 108.8 %copy-start.15 = (bf16[1024,704]{0,1:T(8,128)(2,1)S(1)}, bf16[1024,704]{0,1:T(8,128)(2,1)}, u32[]{:S(2)}) copy-start(bf16[1024,704]{0,1:T(8,128)(2,1)} %param.19) | copy-start | bytes 4325380
  189.8 106.6 %all-gather.5.cloned.1.call-start = ((), (), s32[]{:S(2)}) async-start(), calls=%async_computation.4 | async-start | bytes 2621440 | tf_op jit(solution)/shard_map/all_gather | solution.py:151
  246.1 116.4 %reduce-scatter.5.cloned.1.call-start = ((), (), s32[]{:S(2)}) async-start(), calls=%async_computation.5 | async-start | bytes 2621440 | tf_op jit(solution)/shard_map/reduce_scatter | solution.py:159
  303.4 59.1 %copy-start.1 = (bf16[1024,256]{1,0:T(8,128)(2,1)S(1)}, bf16[1024,256]{1,0:T(8,128)(2,1)}, u32[]{:S(2)}) copy-start(bf16[1024,256]{1,0:T(8,128)(2,1)} %add_convert_fusion.1) | copy-start | bytes 1572868
  (6 other events, 15.6 us)
Sparse Core Ops, SparseCore 0:
  9.1 53.9 all-gather.2
  189.9 54.1 reduce-scatter.2
  246.2 50.1 all-gather.4
  311.4 51.0 reduce-scatter.4
where the time goes:
time: 372 us; the launch traced here: 371 us
  waiting for transfers between devices  214 us (58%)
  starting transfers between devices  68.5 us (18%)
  matrix products  41.4 us (11%)
  other arithmetic  20.5 us (6%)
  between operations  15.1 us (4%)
  local copies, waits for them, and re-layouts  11.4 us (3%)
    ppermute x17, starting transfers between devices, passed_along(): return lax.ppermute(block, axis, route)  68.2 us
    reduce_scatter x1, waiting for transfers between devices, body(): lax.psum_scatter(partial_value.astype(jnp.bfloat16), ('tr', 'tc'), scatte...  54.3 us
    reduce_scatter x1, waiting for transfers between devices, body(): lax.psum_scatter(down.astype(jnp.bfloat16), ('tr', 'tc'), scatter_dimensi...  51.2 us
    all_gather x1, waiting for transfers between devices, body(): piece = lax.all_gather(resid, ('tr', 'tc'), axis=1, tiled=True)  50 us
    all_gather x1, waiting for transfers between devices, body(): piece = lax.all_gather(activations, ('tr', 'tc'), axis=1, tiled=True)  46.8 us
    ppermute x17, waiting for transfers between devices, passed_along(): return lax.ppermute(block, axis, route)  10.9 us
    dot_general x2, matrix products, body(): jnp.einsum('hqk,khd->qhd', probs, values_all, preferred_element_type=jnp....  9.03 us
    dot_general x1, matrix products, body(): down = jnp.dot(hidden, w_down, preferred_element_type=jnp.float32)  7.8 us
  transfers between devices with their start and end apart: 21, of which 10 were waited for; matrix products, arithmetic and copies ran while one was open for 8% of the time, Pallas kernels for 0%

commit v1 on v0

--- a/solution.py
+++ b/solution.py
@@ -75,7 +75,8 @@
     position = row_ids % SEG
     segment_of = row_ids // SEG
     continuing = seg_start[segment_of] == 0
-    piece = lax.all_gather(activations, ("tr", "tc"), axis=1, tiled=True)
+    sent = jnp.stack([activations] * lax.axis_size(("tr", "tc")))
+    piece = jnp.concatenate(lax.all_to_all(sent, ("tr", "tc"), 0, 0), axis=1)
     piece_f = piece.astype(jnp.float32)
     projected = jnp.dot(piece, wide, preferred_element_type=jnp.float32)
     squares = jnp.sum(piece_f * piece_f, -1)

time: 372 us -> 357 us (0.960)
  waiting for transfers between devices: 214 us -> 167 us
  starting transfers between devices: 68.5 us -> 84.1 us
  local copies, waits for them, and re-layouts: 11.4 us -> 20.4 us
  other arithmetic: 20.5 us -> 28.5 us
    all_gather x1 -> x0, waiting for transfers between devices: 46.8 us -> none  [body(): piece = lax.all_gather(activations, ('tr', 'tc'), axis=1, tiled=True)]
    ppermute x17, starting transfers between devices: 68.2 us -> 79 us  [passed_along(): return lax.ppermute(block, axis, route)]
    all_to_all x0 -> x1, waiting for transfers between devices: none -> 7.03 us  [body(): piece = jnp.concatenate(lax.all_to_all(sent, ('tr', 'tc'), 0, 0), axis=1)]
    ppermute x17, waiting for transfers between devices: 10.9 us -> 3.95 us  [passed_along(): return lax.ppermute(block, axis, route)]
    all_to_all x0 -> x1, starting transfers between devices: none -> 4.83 us  [body(): piece = jnp.concatenate(lax.all_to_all(sent, ('tr', 'tc'), 0, 0), axis=1)]
  transfers between devices with their start and end apart: 21 -> 21, of which waited for: 10 -> 6; matrix products, arithmetic and copies ran while one was open for 8% -> 12% of each run, Pallas kernels for 0% -> 0%
where the time goes in v1:
time: 357 us; the launch traced here: 356 us
  waiting for transfers between devices  167 us (47%)
  starting transfers between devices  84.1 us (24%)
  matrix products  40.9 us (11%)
  other arithmetic  28.5 us (8%)
  local copies, waits for them, and re-layouts  20.4 us (6%)
  between operations  15.1 us (4%)
    ppermute x17, starting transfers between devices, passed_along(): return lax.ppermute(block, axis, route)  79 us
    reduce_scatter x1, waiting for transfers between devices, body(): lax.psum_scatter(partial_value.astype(jnp.bfloat16), ('tr', 'tc'), scatte...  54.7 us
    reduce_scatter x1, waiting for transfers between devices, body(): lax.psum_scatter(down.astype(jnp.bfloat16), ('tr', 'tc'), scatter_dimensi...  51.2 us
    all_gather x1, waiting for transfers between devices, body(): piece = lax.all_gather(resid, ('tr', 'tc'), axis=1, tiled=True)  50.1 us
    dot_general x2, matrix products, body(): jnp.einsum('hqk,khd->qhd', probs, values_all, preferred_element_type=jnp....  9.03 us
    dot_general x1, matrix products, body(): down = jnp.dot(hidden, w_down, preferred_element_type=jnp.float32)  7.79 us
    add x1, other arithmetic, body(): convolved + jnp.where(valid[:, None], taps[offset] * shifted, 0.0)  7.24 us
  transfers between devices with their start and end apart: 21, of which 6 were waited for; matrix products, arithmetic and copies ran while one was open for 12% of the time, Pallas kernels for 0%

profile of v1, /device:TPU:1, one launch (start us, length us, event | category | flops | bytes accessed | tf_op | source)
XLA Modules:
  0.0 356.1 jit_solution(9158407504251448679)
XLA Ops:
  9.5 4.8 %all-to-all-start = ((bf16[4,1024,256]{1,2,0:T(8,128)(2,1)}), bf16[4,1024,256]{1,2,0:T(8,128)(2,1)S(1)}, u32[]{:S(2)}, u32[]{:S(2)}) async-start(bf16[4,1024,256]{1,2,0:T(8,128)(2,1)} %stack.2), calls=%async_computation | async-start | bytes 4194304 | tf_op jit(solution)/shard_map/all_to_all | solution.py:79
  22.0 2.6 copy.79
  30.8 2.7 fusion.7
  33.5 7.0 %all-to-all-done = bf16[4,1024,256]{1,2,0:T(8,128)(2,1)S(1)} async-done(((bf16[4,1024,256]{1,2,0:T(8,128)(2,1)}), bf16[4,1024,256]{1,2,0:T(8,128)(2,1)S(1)}, u32[]{:S(2)}, u32[]{:S(2)}) %all-to-all-start) | async-done | bytes 2097184 | tf_op jit(solution)/shard_map/all_to_all | solution.py:79
  41.1 3.3 multiply_convert_fusion
  45.6 4.2 %collective-permute-start = (bf16[3,768]{1,0:T(4,128)(2,1)S(1)}, bf16[3,768]{1,0:T(4,128)(2,1)S(1)}, u32[]{:S(2)}, u32[]{:S(2)}) collective-permute-start(bf16[3,768]{1,0:T(4,128)(2,1)S(1)} %slice.81), channel_id=1, source_target_pairs={{0,4},{4,8},{8,12},{12,16},{16,20},{20,24},{24,28},{28,32},{32,36}... | collective-permute-start | bytes 13832 | tf_op jit(solution)/shard_map/ppermute | solution.py:17
  51.2 7.2 %select_add_fusion = f32[1024,768]{1,0:T(8,128)} fusion(bf16[1024,768]{1,0:T(8,128)(2,1)} %copy-done.3, bf16[3,768]{1,0:T(4,128)(2,1)S(1)} %collective-permute-done, f32[768]{0:T(1024)S(1)} %mul.252, f32[768]{0:T(1024)S(1)} %mul.249, f32[768]{0:T(1024)S(1)} %mul.246, f32[768]{0:T(1024)S(1)} %mul.240, pred[1024]{0:T(1024)(128)(4,1)} %get-tuple-element.48, ...), kind=kLoop, calls=%fused_computation.10 | loop fusion | flops 18874368 | bytes 4739584 | tf_op jit(solution)/shard_map/add | solution.py:91
  58.5 5.2 %reshape.308 = f32[1024,3,2,128]{3,2,1,0:T(2,128)} reshape(f32[1024,768]{1,0:T(8,128)} %select_add_fusion) | data formatting | bytes 6291456 | tf_op jit(solution)/shard_map/reshape | solution.py:92
  69.8 3.4 collective-permute-start.5
  73.2 2.4 collective-permute-start.6
  77.1 3.6 %collective-permute-start.1 = (bf16[2,256,256]{1,2,0:T(8,128)(2,1)}, bf16[2,256,256]{1,2,0:T(8,128)(2,1)S(1)}, u32[]{:S(2)}, u32[]{:S(2)}) collective-permute-start(bf16[2,256,256]{1,2,0:T(8,128)(2,1)} %fusion.18), channel_id=1, source_target_pairs={{0,4},{4,8},{8,12},{12,16},{16,20},{20,24},{24,28},{28,32},{32,36}... | collective-permute-start | bytes 786440 | tf_op jit(solution)/shard_map/ppermute | solution.py:17
  80.7 3.0 fusion.3
  83.8 3.0 fusion.1
  86.7 4.5 %fusion.12 = f32[512,2,128]{0,2,1:T(8,128)S(1)} fusion(f32[2,512,1040]{1,2,0:T(8,128)} %fusion.3, bf16[1024,2,128]{2,0,1:T(8,128)(2,1)} %bitcast.89, bf16[16,2,128]{2,0,1:T(8,128)(2,1)S(1)} %copy.81), kind=kOutput, calls=%fused_computation.29 | convolution fusion | flops 275826688 | bytes 5316608 | tf_op jit(solution)/shard_map/hqk,khd->qhd/dot_general | solution.py:143
  92.7 3.6 collective-permute-start.8
  96.3 6.0 %collective-permute-start.7 = (bf16[2,256,128]{1,2,0:T(8,128)(2,1)S(1)}, bf16[2,256,128]{1,2,0:T(8,128)(2,1)S(1)}, u32[]{:S(2)}, u32[]{:S(2)}) collective-permute-start(bf16[2,256,128]{1,2,0:T(8,128)(2,1)S(1)} %get-tuple-element.18), channel_id=1, source_target_pairs={{0,8},{4,12},{8,16},{12,20},{16,24},{20,28},{24,32},{28,36},{32,40... | collective-permute-start | bytes 393224 | tf_op jit(solution)/shard_map/ppermute | solution.py:17
  105.6 3.7 %collective-permute-start.10 = (bf16[2,256,128]{1,2,0:T(8,128)(2,1)S(1)}, bf16[2,256,128]{1,2,0:T(8,128)(2,1)S(1)}, u32[]{:S(2)}, u32[]{:S(2)}) collective-permute-start(bf16[2,256,128]{1,2,0:T(8,128)(2,1)S(1)} %get-tuple-element.15), channel_id=1, source_target_pairs={{0,16},{4,20},{8,24},{12,28},{16,32},{20,36},{24,40},{28,44},{32,4... | collective-permute-start | bytes 393224 | tf_op jit(solution)/shard_map/ppermute | solution.py:17
  109.2 4.8 %collective-permute-start.9 = (bf16[2,256,128]{1,2,0:T(8,128)(2,1)S(1)}, bf16[2,256,128]{1,2,0:T(8,128)(2,1)S(1)}, u32[]{:S(2)}, u32[]{:S(2)}) collective-permute-start(bf16[2,256,128]{1,2,0:T(8,128)(2,1)S(1)} %get-tuple-element.16), channel_id=1, source_target_pairs={{0,16},{4,20},{8,24},{12,28},{16,32},{20,36},{24,40},{28,44},{32,4... | collective-permute-start | bytes 393224 | tf_op jit(solution)/shard_map/ppermute | solution.py:17
  118.4 8.6 %collective-permute-start.12 = (bf16[2,256,128]{1,2,0:T(8,128)(2,1)S(1)}, bf16[2,256,128]{1,2,0:T(8,128)(2,1)S(1)}, u32[]{:S(2)}, u32[]{:S(2)}) collective-permute-start(bf16[2,256,128]{1,2,0:T(8,128)(2,1)S(1)} %get-tuple-element.13), channel_id=1, source_target_pairs={{0,32},{4,36},{8,40},{12,44},{16,48},{20,52},{24,56},{28,60},{32,6... | collective-permute-start | bytes 393224 | tf_op jit(solution)/shard_map/ppermute | solution.py:17
  127.0 5.2 %collective-permute-start.11 = (bf16[2,256,128]{1,2,0:T(8,128)(2,1)S(1)}, bf16[2,256,128]{1,2,0:T(8,128)(2,1)S(1)}, u32[]{:S(2)}, u32[]{:S(2)}) collective-permute-start(bf16[2,256,128]{1,2,0:T(8,128)(2,1)S(1)} %get-tuple-element.14), channel_id=1, source_target_pairs={{0,32},{4,36},{8,40},{12,44},{16,48},{20,52},{24,56},{28,60},{32,6... | collective-permute-start | bytes 393224 | tf_op jit(solution)/shard_map/ppermute | solution.py:17
  132.6 6.9 %collective-permute-start.4 = (bf16[2,256,256]{2,1,0:T(8,128)(2,1)S(1)}, bf16[2,256,256]{2,1,0:T(8,128)(2,1)S(1)}, u32[]{:S(2)}, u32[]{:S(2)}) collective-permute-start(bf16[2,256,256]{2,1,0:T(8,128)(2,1)S(1)} %get-tuple-element.40), channel_id=1, source_target_pairs={{0,32},{4,36},{8,40},{12,44},{16,48},{20,52},{24,56},{28,60},{32,6... | collective-permute-start | bytes 786440 | tf_op jit(solution)/shard_map/ppermute | solution.py:17
  140.2 8.9 %collective-permute-start.14 = (bf16[2,256,128]{1,2,0:T(8,128)(2,1)S(1)}, bf16[2,256,128]{1,2,0:T(8,128)(2,1)S(1)}, u32[]{:S(2)}, u32[]{:S(2)}) collective-permute-start(bf16[2,256,128]{1,2,0:T(8,128)(2,1)S(1)} %get-tuple-element.11), channel_id=1, source_target_pairs={{0,64},{4,68},{8,72},{12,76},{16,80},{20,84},{24,88},{28,92},{32,9... | collective-permute-start | bytes 393224 | tf_op jit(solution)/shard_map/ppermute | solution.py:17
  149.1 3.2 collective-permute-start.13
  152.3 2.6 collective-permute-done.4
  156.1 8.8 %collective-permute-start.16 = (bf16[2,128,128]{1,2,0:T(8,128)(2,1)S(1)}, bf16[2,128,128]{1,2,0:T(8,128)(2,1)S(1)}, u32[]{:S(2)}, u32[]{:S(2)}) collective-permute-start(bf16[2,128,128]{1,2,0:T(8,128)(2,1)S(1)} %get-tuple-element.9), channel_id=1, source_target_pairs={{0,4},{4,8},{8,12},{12,16},{16,20},{20,24},{24,28},{28,32},{32,36}... | collective-permute-start | bytes 196616 | tf_op jit(solution)/shard_map/ppermute | solution.py:17
  166.8 4.5 %fusion.13 = f32[512,2,128]{0,2,1:T(8,128)S(1)} fusion(f32[2,512,1040]{1,2,0:T(8,128)} %fusion.1, bf16[1024,2,128]{2,0,1:T(8,128)(2,1)} %bitcast.90, bf16[16,2,128]{2,0,1:T(8,128)(2,1)S(1)} %copy.81), kind=kOutput, calls=%fused_computation.30 | convolution fusion | flops 275826688 | bytes 5316608 | tf_op jit(solution)/shard_map/hqk,khd->qhd/dot_general | solution.py:143
  172.4 2.1 convolution_convert_fusion
  174.6 54.7 %reduce-scatter.3.cloned.1.call-done = bf16[1024,256]{1,0:T(8,128)(2,1)} async-done(((bf16[1024,1024]{1,0:T(8,128)(2,1)}), bf16[1024,256]{1,0:T(8,128)(2,1)}) %reduce-scatter.3.cloned.1.call-update) | async-done | bytes 524304 | tf_op jit(solution)/shard_map/reduce_scatter | solution.py:148
  231.5 50.1 %all-gather.2.cloned.1.call-done = bf16[1024,1024]{1,0:T(8,128)(2,1)} async-done(((bf16[1024,256]{1,0:T(8,128)(2,1)}), bf16[1024,1024]{1,0:T(8,128)(2,1)}) %all-gather.2.cloned.1.call-update) | async-done | bytes 2097168 | tf_op jit(solution)/shard_map/all_gather | solution.py:152
  283.6 4.9 %fusion.91 = f32[1024,704]{0,1:T(8,128)} fusion(bf16[1024,1024]{1,0:T(8,128)(2,1)} %all-gather.2.cloned.1.call-done, bf16[1024,704]{0,1:T(8,128)(2,1)S(1)} %copy-done.19), kind=kOutput, calls=%fused_computation.159 | convolution fusion | flops 1476395008 | bytes 6422528 | tf_op jit(solution)/shard_map/dot_general | solution.py:154
  288.5 7.8 %convolution_convert_fusion.1 = bf16[1024,1024]{1,0:T(8,128)(2,1)} fusion(bf16[704,1024]{1,0:T(8,128)(2,1)S(1)} %copy-done, f32[1024,704]{0,1:T(8,128)} %fusion.91, bf16[1024,1024]{1,0:T(8,128)(2,1)} %all-gather.2.cloned.1.call-done, bf16[1024,704]{0,1:T(8,128)(2,1)} %param.20, f32[1024]{0:T(1024)S(1)} %add_rsqrt_fusion.3), kind=kOutput, calls=%fused_computation.22 | convolution fusion | flops 2959605760 | bytes 9965568 | tf_op jit(solution)/shard_map/dot_general | solution.py:159
  296.3 51.2 %reduce-scatter.5.cloned.1.call-done = bf16[1024,256]{1,0:T(8,128)(2,1)} async-done(((bf16[1024,1024]{1,0:T(8,128)(2,1)}), bf16[1024,256]{1,0:T(8,128)(2,1)}) %reduce-scatter.5.cloned.1.call-update) | async-done | bytes 524304 | tf_op jit(solution)/shard_map/reduce_scatter | solution.py:160
  (125 shorter events, 46.6 us)
Async XLA Ops:
  6.5 282.0 %copy-start = (bf16[704,1024]{1,0:T(8,128)(2,1)S(1)}, bf16[704,1024]{1,0:T(8,128)(2,1)}, u32[]{:S(2)}) copy-start(bf16[704,1024]{1,0:T(8,128)(2,1)} %param.21) | copy-start | bytes 4325380
  7.9 10.7 %copy-start.14 = (bf16[2,16,256]{2,1,0:T(8,128)(2,1)S(1)}, bf16[2,16,256]{2,1,0:T(8,128)(2,1)}, u32[]{:S(2)}) copy-start(bf16[2,16,256]{2,1,0:T(8,128)(2,1)} %param.17) | copy-start | bytes 49156
  9.5 31.0 %all-to-all-start = ((bf16[4,1024,256]{1,2,0:T(8,128)(2,1)}), bf16[4,1024,256]{1,2,0:T(8,128)(2,1)S(1)}, u32[]{:S(2)}, u32[]{:S(2)}) async-start(bf16[4,1024,256]{1,2,0:T(8,128)(2,1)} %stack.2), calls=%async_computation | async-start | bytes 4194304 | tf_op jit(solution)/shard_map/all_to_all | solution.py:79
  14.3 214.9 %reduce-scatter.3.cloned.1.call-start = ((), (), s32[]{:S(2)}) async-start(), calls=%async_computation.3 | async-start | bytes 2621440 | tf_op jit(solution)/shard_map/reduce_scatter | solution.py:148
  41.0 10.1 %copy-start.13 = (f32[3,256]{1,0:T(4,128)S(1)}, f32[3,256]{1,0:T(4,128)}, u32[]{:S(2)}) copy-start(f32[3,256]{1,0:T(4,128)} %get-tuple-element.7) | copy-start | bytes 9220
  41.0 10.2 %copy-start.12 = (f32[3,256]{1,0:T(4,128)S(1)}, f32[3,256]{1,0:T(4,128)}, u32[]{:S(2)}) copy-start(f32[3,256]{1,0:T(4,128)} %get-tuple-element.8) | copy-start | bytes 9220
  41.0 10.2 %copy-start.11 = (bf16[1,16,256]{2,1,0:T(8,128)(2,1)S(1)}, bf16[1,16,256]{2,1,0:T(8,128)(2,1)}, u32[]{:S(2)}) copy-start(bf16[1,16,256]{2,1,0:T(8,128)(2,1)} %get-tuple-element.27) | copy-start | bytes 24580
  45.6 5.7 %collective-permute-start = (bf16[3,768]{1,0:T(4,128)(2,1)S(1)}, bf16[3,768]{1,0:T(4,128)(2,1)S(1)}, u32[]{:S(2)}, u32[]{:S(2)}) collective-permute-start(bf16[3,768]{1,0:T(4,128)(2,1)S(1)} %slice.81), channel_id=1, source_target_pairs={{0,4},{4,8},{8,12},{12,16},{16,20},{20,24},{24,28},{28,32},{32,36}... | collective-permute-start | bytes 13832 | tf_op jit(solution)/shard_map/ppermute | solution.py:17
  67.8 8.5 %copy-start.6 = (f32[1,2,128,128]{2,3,1,0:T(8,128)S(1)}, f32[1,2,128,128]{2,3,1,0:T(8,128)}, u32[]{:S(2)}) copy-start(f32[1,2,128,128]{2,3,1,0:T(8,128)} %broadcast_multiply_fusion) | copy-start | bytes 393220
  69.0 11.7 %copy-start.5 = (pred[512,1040]{0,1:T(8,128)(4,1)S(1)}, pred[512,1040]{0,1:T(8,128)(4,1)}, u32[]{:S(2)}) copy-start(pred[512,1040]{0,1:T(8,128)(4,1)} %get-tuple-element.30) | copy-start | bytes 1597444
  69.0 11.7 %copy-start.15 = (bf16[16,2,128]{2,0,1:T(8,128)(2,1)S(1)}, bf16[16,2,128]{2,0,1:T(8,128)(2,1)}, u32[]{:S(2)}) copy-start(bf16[16,2,128]{2,0,1:T(8,128)(2,1)} %fusion.52) | copy-start | bytes 24580
  69.8 21.5 %collective-permute-start.5 = (bf16[2,256,128]{1,2,0:T(8,128)(2,1)}, bf16[2,256,128]{1,2,0:T(8,128)(2,1)}, u32[]{:S(2)}, u32[]{:S(2)}) collective-permute-start(bf16[2,256,128]{1,2,0:T(8,128)(2,1)} %fusion.24), channel_id=1, source_target_pairs={{0,4},{4,8},{8,12},{12,16},{16,20},{20,24},{24,28},{28,32},{32,36}... | collective-permute-start | bytes 393224 | tf_op jit(solution)/shard_map/ppermute | solution.py:17
  73.2 18.0 %collective-permute-start.6 = (bf16[2,256,128]{1,2,0:T(8,128)(2,1)S(1)}, bf16[2,256,128]{1,2,0:T(8,128)(2,1)}, u32[]{:S(2)}, u32[]{:S(2)}) collective-permute-start(bf16[2,256,128]{1,2,0:T(8,128)(2,1)S(1)} %fusion.25), channel_id=1, source_target_pairs={{0,4},{4,8},{8,12},{12,16},{16,20},{20,24},{24,28},{28,32},{32,36}... | collective-permute-start | bytes 393224 | tf_op jit(solution)/shard_map/ppermute | solution.py:17
  77.1 25.2 %collective-permute-start.1 = (bf16[2,256,256]{1,2,0:T(8,128)(2,1)}, bf16[2,256,256]{1,2,0:T(8,128)(2,1)S(1)}, u32[]{:S(2)}, u32[]{:S(2)}) collective-permute-start(bf16[2,256,256]{1,2,0:T(8,128)(2,1)} %fusion.18), channel_id=1, source_target_pairs={{0,4},{4,8},{8,12},{12,16},{16,20},{20,24},{24,28},{28,32},{32,36}... | collective-permute-start | bytes 786440 | tf_op jit(solution)/shard_map/ppermute | solution.py:17
  92.7 12.1 %collective-permute-start.8 = (bf16[2,256,128]{1,2,0:T(8,128)(2,1)S(1)}, bf16[2,256,128]{1,2,0:T(8,128)(2,1)S(1)}, u32[]{:S(2)}, u32[]{:S(2)}) collective-permute-start(bf16[2,256,128]{1,2,0:T(8,128)(2,1)S(1)} %get-tuple-element.17), channel_id=1, source_target_pairs={{0,8},{4,12},{8,16},{12,20},{16,24},{20,28},{24,32},{28,36},{32,40... | collective-permute-start | bytes 393224 | tf_op jit(solution)/shard_map/ppermute | solution.py:17
  96.3 8.6 %collective-permute-start.7 = (bf16[2,256,128]{1,2,0:T(8,128)(2,1)S(1)}, bf16[2,256,128]{1,2,0:T(8,128)(2,1)S(1)}, u32[]{:S(2)}, u32[]{:S(2)}) collective-permute-start(bf16[2,256,128]{1,2,0:T(8,128)(2,1)S(1)} %get-tuple-element.18), channel_id=1, source_target_pairs={{0,8},{4,12},{8,16},{12,20},{16,24},{20,28},{24,32},{28,36},{32,40... | collective-permute-start | bytes 393224 | tf_op jit(solution)/shard_map/ppermute | solution.py:17
  102.9 11.1 %collective-permute-start.2 = (bf16[2,256,256]{2,1,0:T(8,128)(2,1)S(1)}, bf16[2,256,256]{2,1,0:T(8,128)(2,1)S(1)}, u32[]{:S(2)}, u32[]{:S(2)}) collective-permute-start(bf16[2,256,256]{2,1,0:T(8,128)(2,1)S(1)} %get-tuple-element.34), channel_id=1, source_target_pairs={{0,8},{4,12},{8,16},{12,20},{16,24},{20,28},{24,32},{28,36},{32,40... | collective-permute-start | bytes 786440 | tf_op jit(solution)/shard_map/ppermute | solution.py:17
  105.6 10.8 %collective-permute-start.10 = (bf16[2,256,128]{1,2,0:T(8,128)(2,1)S(1)}, bf16[2,256,128]{1,2,0:T(8,128)(2,1)S(1)}, u32[]{:S(2)}, u32[]{:S(2)}) collective-permute-start(bf16[2,256,128]{1,2,0:T(8,128)(2,1)S(1)} %get-tuple-element.15), channel_id=1, source_target_pairs={{0,16},{4,20},{8,24},{12,28},{16,32},{20,36},{24,40},{28,44},{32,4... | collective-permute-start | bytes 393224 | tf_op jit(solution)/shard_map/ppermute | solution.py:17
  109.2 8.5 %collective-permute-start.9 = (bf16[2,256,128]{1,2,0:T(8,128)(2,1)S(1)}, bf16[2,256,128]{1,2,0:T(8,128)(2,1)S(1)}, u32[]{:S(2)}, u32[]{:S(2)}) collective-permute-start(bf16[2,256,128]{1,2,0:T(8,128)(2,1)S(1)} %get-tuple-element.16), channel_id=1, source_target_pairs={{0,16},{4,20},{8,24},{12,28},{16,32},{20,36},{24,40},{28,44},{32,4... | collective-permute-start | bytes 393224 | tf_op jit(solution)/shard_map/ppermute | solution.py:17
  114.4 17.7 %collective-permute-start.3 = (bf16[2,256,256]{2,1,0:T(8,128)(2,1)S(1)}, bf16[2,256,256]{2,1,0:T(8,128)(2,1)S(1)}, u32[]{:S(2)}, u32[]{:S(2)}) collective-permute-start(bf16[2,256,256]{2,1,0:T(8,128)(2,1)S(1)} %get-tuple-element.37), channel_id=1, source_target_pairs={{0,16},{4,20},{8,24},{12,28},{16,32},{20,36},{24,40},{28,44},{32,4... | collective-permute-start | bytes 786440 | tf_op jit(solution)/shard_map/ppermute | solution.py:17
  118.4 21.1 %collective-permute-start.12 = (bf16[2,256,128]{1,2,0:T(8,128)(2,1)S(1)}, bf16[2,256,128]{1,2,0:T(8,128)(2,1)S(1)}, u32[]{:S(2)}, u32[]{:S(2)}) collective-permute-start(bf16[2,256,128]{1,2,0:T(8,128)(2,1)S(1)} %get-tuple-element.13), channel_id=1, source_target_pairs={{0,32},{4,36},{8,40},{12,44},{16,48},{20,52},{24,56},{28,60},{32,6... | collective-permute-start | bytes 393224 | tf_op jit(solution)/shard_map/ppermute | solution.py:17
  127.0 12.5 %collective-permute-start.11 = (bf16[2,256,128]{1,2,0:T(8,128)(2,1)S(1)}, bf16[2,256,128]{1,2,0:T(8,128)(2,1)S(1)}, u32[]{:S(2)}, u32[]{:S(2)}) collective-permute-start(bf16[2,256,128]{1,2,0:T(8,128)(2,1)S(1)} %get-tuple-element.14), channel_id=1, source_target_pairs={{0,32},{4,36},{8,40},{12,44},{16,48},{20,52},{24,56},{28,60},{32,6... | collective-permute-start | bytes 393224 | tf_op jit(solution)/shard_map/ppermute | solution.py:17
  132.6 22.4 %collective-permute-start.4 = (bf16[2,256,256]{2,1,0:T(8,128)(2,1)S(1)}, bf16[2,256,256]{2,1,0:T(8,128)(2,1)S(1)}, u32[]{:S(2)}, u32[]{:S(2)}) collective-permute-start(bf16[2,256,256]{2,1,0:T(8,128)(2,1)S(1)} %get-tuple-element.40), channel_id=1, source_target_pairs={{0,32},{4,36},{8,40},{12,44},{16,48},{20,52},{24,56},{28,60},{32,6... | collective-permute-start | bytes 786440 | tf_op jit(solution)/shard_map/ppermute | solution.py:17
  140.2 15.1 %collective-permute-start.14 = (bf16[2,256,128]{1,2,0:T(8,128)(2,1)S(1)}, bf16[2,256,128]{1,2,0:T(8,128)(2,1)S(1)}, u32[]{:S(2)}, u32[]{:S(2)}) collective-permute-start(bf16[2,256,128]{1,2,0:T(8,128)(2,1)S(1)} %get-tuple-element.11), channel_id=1, source_target_pairs={{0,64},{4,68},{8,72},{12,76},{16,80},{20,84},{24,88},{28,92},{32,9... | collective-permute-start | bytes 393224 | tf_op jit(solution)/shard_map/ppermute | solution.py:17
  149.1 6.2 %collective-permute-start.13 = (bf16[2,256,128]{1,2,0:T(8,128)(2,1)S(1)}, bf16[2,256,128]{1,2,0:T(8,128)(2,1)S(1)}, u32[]{:S(2)}, u32[]{:S(2)}) collective-permute-start(bf16[2,256,128]{1,2,0:T(8,128)(2,1)S(1)} %get-tuple-element.12), channel_id=1, source_target_pairs={{0,64},{4,68},{8,72},{12,76},{16,80},{20,84},{24,88},{28,92},{32,9... | collective-permute-start | bytes 393224 | tf_op jit(solution)/shard_map/ppermute | solution.py:17
  156.1 15.3 %collective-permute-start.16 = (bf16[2,128,128]{1,2,0:T(8,128)(2,1)S(1)}, bf16[2,128,128]{1,2,0:T(8,128)(2,1)S(1)}, u32[]{:S(2)}, u32[]{:S(2)}) collective-permute-start(bf16[2,128,128]{1,2,0:T(8,128)(2,1)S(1)} %get-tuple-element.9), channel_id=1, source_target_pairs={{0,4},{4,8},{8,12},{12,16},{16,20},{20,24},{24,28},{28,32},{32,36}... | collective-permute-start | bytes 196616 | tf_op jit(solution)/shard_map/ppermute | solution.py:17
  164.9 6.5 %collective-permute-start.15 = (bf16[2,128,128]{1,2,0:T(8,128)(2,1)S(1)}, bf16[2,128,128]{1,2,0:T(8,128)(2,1)S(1)}, u32[]{:S(2)}, u32[]{:S(2)}) collective-permute-start(bf16[2,128,128]{1,2,0:T(8,128)(2,1)S(1)} %get-tuple-element.10), channel_id=1, source_target_pairs={{0,4},{4,8},{8,12},{12,16},{16,20},{20,24},{24,28},{28,32},{32,36}... | collective-permute-start | bytes 196616 | tf_op jit(solution)/shard_map/ppermute | solution.py:17
  172.3 57.0 %copy-start.2 = (bf16[1024,256]{1,0:T(8,128)(2,1)S(1)}, bf16[1024,256]{1,0:T(8,128)(2,1)}, u32[]{:S(2)}) copy-start(bf16[1024,256]{1,0:T(8,128)(2,1)} %param.11) | copy-start | bytes 1572868
  174.5 109.1 %copy-start.19 = (bf16[1024,704]{0,1:T(8,128)(2,1)S(1)}, bf16[1024,704]{0,1:T(8,128)(2,1)}, u32[]{:S(2)}) copy-start(bf16[1024,704]{0,1:T(8,128)(2,1)} %param.19) | copy-start | bytes 4325380
  174.5 107.0 %all-gather.2.cloned.1.call-start = ((), (), s32[]{:S(2)}) async-start(), calls=%async_computation.4 | async-start | bytes 2621440 | tf_op jit(solution)/shard_map/all_gather | solution.py:152
  231.2 116.4 %reduce-scatter.5.cloned.1.call-start = ((), (), s32[]{:S(2)}) async-start(), calls=%async_computation.5 | async-start | bytes 2621440 | tf_op jit(solution)/shard_map/reduce_scatter | solution.py:160
  288.5 59.1 %copy-start.1 = (bf16[1024,256]{1,0:T(8,128)(2,1)S(1)}, bf16[1024,256]{1,0:T(8,128)(2,1)}, u32[]{:S(2)}) copy-start(bf16[1024,256]{1,0:T(8,128)(2,1)} %add_convert_fusion.1) | copy-start | bytes 1572868
  (9 other events, 36.2 us)
Sparse Core Ops, SparseCore 0:
  174.6 54.5 reduce-scatter.2
  231.3 50.1 all-gather.1
  296.5 51.0 reduce-scatter.4
